TPU v7x, 512 devices: a whole 4x8x8 slice. The times are simulated.
512 devices in a mesh: patch: 128 (over y, z_lo, x), chan: 4 (over z_hi, core).
Axes of the slice: x: 4, y: 8, z: 8 (z_hi: 2, z_lo: 4; z = z_hi * 4 + z_lo), core: 2. Of those that a mesh axis runs over, the one named last changes fastest.
Arguments:
- latent: bfloat16 [8192, 1280], P('patch', 'chan'), may hold values from -6 to 6
- timestep: int32 [1], replicated, may hold values from 0 to 999
- norm_gain: float32 [1280], P('chan'), may hold values from 0.25 to 1.75
- norm_bias: float32 [1280], P('chan'), may hold values from -3 to 3
- w_time: bfloat16 [320, 1280], P(None, 'chan'), may hold values from -0.3125 to 0.3125
- w_query: bfloat16 [1280, 1024], P(None, 'chan'), may hold values from -0.15625 to 0.15625
- w_key: bfloat16 [1280, 1024], P(None, 'chan'), may hold values from -0.3125 to 0.3125
- w_value: bfloat16 [1280, 1024], P(None, 'chan'), may hold values from -0.15625 to 0.15625
- w_out: bfloat16 [1024, 1280], P('chan'), may hold values from -0.1875 to 0.1875
- stale_keys: bfloat16 [8192, 1024], P('patch', 'chan'), may hold values from -12 to 12
- stale_values: bfloat16 [8192, 1024], P('patch', 'chan'), may hold values from -6 to 6
Outputs:
- mixed: bfloat16 [8192, 1280], P('patch', 'chan')
- fresh_keys: bfloat16 [8192, 1024], P('patch', 'chan')
- fresh_values: bfloat16 [8192, 1024], P('patch', 'chan')
All inputs are finite; a program needn't handle non-finite values.
Results may differ from a plain program's by a relative error of at most 0.006.
Values may be sent and summed in bfloat16 or wider, within the bound.
No kernel may reach another device: no remote copies, remote signals or barrier semaphores. Data moves between devices by JAX's collectives and lax.ppermute only.
A program may use at most 64 MiB of HBM per device.

v0:
```python
import math
import jax
import jax.numpy as jnp
from jax import lax
from jax.sharding import PartitionSpec as P

D = 1280
HEAD_DIM = 64
GROUPS = 32


def timestep_shift(timestep, w_time):
    half_dim = w_time.shape[0] // 2
    frequency = jnp.exp(-math.log(10000.0) * jnp.arange(half_dim, dtype=jnp.float32) / half_dim)
    angles = timestep[0].astype(jnp.float32) * frequency
    embedding = jnp.concatenate([jnp.cos(angles), jnp.sin(angles)])
    return jnp.dot(
        jax.nn.silu(embedding)[None, :], w_time.astype(jnp.float32), precision=lax.Precision.HIGHEST
    )[0]


def local(
    latent,
    timestep,
    norm_gain,
    norm_bias,
    w_time,
    w_query,
    w_key,
    w_value,
    w_out,
    stale_keys,
    stale_values,
):
    rows_here, chan_width = latent.shape
    patch_count = lax.axis_size("patch")
    chan_count = lax.axis_size("chan")
    device = lax.axis_index("patch")
    local_groups = GROUPS // chan_count
    width = D // GROUPS
    values = latent.astype(jnp.float32).reshape(rows_here, local_groups, width)
    amount = rows_here * patch_count * width
    group_total = lax.psum(jnp.sum(values, axis=(0, 2)), "patch")
    group_mean = group_total / amount
    centered = values - group_mean[None, :, None]
    spread = lax.psum(jnp.sum(centered * centered, axis=(0, 2)), "patch")
    variance = spread / amount
    scaled = (centered * lax.rsqrt(variance + 1e-05)[None, :, None]).reshape(rows_here, chan_width)
    normed = (scaled * norm_gain + norm_bias + timestep_shift(timestep, w_time)).astype(
        jnp.bfloat16
    )
    inner = w_query.shape[1]
    shard_piece = lax.all_gather(normed, "chan", axis=1, tiled=True)
    outputs = []
    for index, weight_matrix in enumerate((w_query, w_key, w_value)):
        outputs.append(jnp.dot(shard_piece, weight_matrix, preferred_element_type=jnp.float32))
    summed = tuple(outputs)
    queries = summed[0].astype(jnp.bfloat16)
    fresh_keys = summed[1].astype(jnp.bfloat16)
    fresh_values = summed[2].astype(jnp.bfloat16)
    heads_here = inner // HEAD_DIM
    score_scale = HEAD_DIM ** (-0.5)
    query_heads = queries.reshape(rows_here, heads_here, HEAD_DIM)

    def slab_stats(key_block, value_block):
        score = (
            jnp.einsum("qhd,skhd->hqsk", query_heads, key_block, preferred_element_type=jnp.float32)
            * score_scale
        )
        block_max = jnp.max(score, axis=-1)
        weight = jnp.exp(score - block_max[..., None]).astype(jnp.bfloat16)
        block_num = jnp.einsum(
            "hqsk,skhd->hqsd", weight, value_block, preferred_element_type=jnp.float32
        )
        block_den = jnp.sum(weight.astype(jnp.float32), axis=-1)
        return (block_max, block_num, block_den)

    def combine(running, block_max, block_num, block_den):
        run_max, run_num, run_den = running
        new_max = jnp.maximum(run_max, jnp.max(block_max, axis=-1))
        keep_old = jnp.exp(run_max - new_max)
        factor = jnp.exp(block_max - new_max[..., None])
        run_num = keep_old[..., None] * run_num + jnp.sum(factor[..., None] * block_num, axis=2)
        run_den = keep_old * run_den + jnp.sum(factor * block_den, axis=2)
        return (new_max, run_num, run_den)

    home_max, home_num, home_den = slab_stats(
        fresh_keys.reshape(1, rows_here, heads_here, HEAD_DIM),
        fresh_values.reshape(1, rows_here, heads_here, HEAD_DIM),
    )
    start_state = (home_max[..., 0], home_num[:, :, 0], home_den[..., 0])
    key_piece = lax.all_gather(stale_keys, "patch", axis=0, tiled=True)
    value_piece = lax.all_gather(stale_values, "patch", axis=0, tiled=True)
    slab_count = key_piece.shape[0] // rows_here
    per_step = math.gcd(slab_count, 8)
    key_steps = key_piece.reshape(slab_count // per_step, per_step, rows_here, heads_here, HEAD_DIM)
    value_steps = value_piece.reshape(
        slab_count // per_step, per_step, rows_here, heads_here, HEAD_DIM
    )

    def advance(state, inputs):
        key_block, value_block, index = inputs
        block_max, block_num, block_den = slab_stats(key_block, value_block)
        slab_ids = index * per_step + jnp.arange(per_step, dtype=jnp.int32)
        is_home = slab_ids == device
        block_max = jnp.where(is_home[None, None, :], -1e30, block_max)
        return (combine(state, block_max, block_num, block_den), None)

    step_ids = jnp.arange(slab_count // per_step, dtype=jnp.int32)
    result, unused = lax.scan(advance, start_state, (key_steps, value_steps, step_ids))
    final_max, final_num, final_den = result
    attended = (
        jnp.transpose(final_num / final_den[..., None], (1, 0, 2))
        .reshape(rows_here, inner)
        .astype(jnp.bfloat16)
    )
    projected = lax.psum_scatter(
        jnp.dot(attended, w_out, preferred_element_type=jnp.float32).T,
        "chan",
        scatter_dimension=0,
        tiled=True,
    ).T
    mixed = (latent.astype(jnp.float32) + projected).astype(jnp.bfloat16)
    return (mixed, fresh_keys, fresh_values)


def solution(mesh):
    in_specs = (
        P("patch", "chan"),
        P(),
        P("chan"),
        P("chan"),
        P(None, "chan"),
        P(None, "chan"),
        P(None, "chan"),
        P(None, "chan"),
        P("chan", None),
        P("patch", "chan"),
        P("patch", "chan"),
    )
    out_specs = (P("patch", "chan"), P("patch", "chan"), P("patch", "chan"))
    return jax.shard_map(local, mesh=mesh, in_specs=in_specs, out_specs=out_specs, check_vma=False)
```

profile of v0, /device:TPU:1, one launch (start us, length us, event | category | flops | bytes accessed | tf_op | source)
XLA Modules:
  0.0 1531.6 jit_solution(9358067000586807633)
XLA Ops:
  7.2 0.7 all-gather.4.cloned.1.call-update
  8.0 0.7 all-gather.6.cloned.1.call-update
  8.7 0.8 convert_reduce_fusion.1
  9.7 319.5 %psum.14 = f32[8]{0:T(128)S(1)} all-reduce(f32[8]{0:T(128)S(1)} %reduce_sum.70), channel_id=1, replica_groups=mesh['patch'=128,'chan'=4] {'patch'}, use_global_device_ids=true, to_apply=%region_2.0 | all-reduce | flops 8 | bytes 64 | tf_op jit(solution)/shard_map/psum | solution.py:43
  329.4 0.8 fusion.7
  330.4 309.2 %psum.15 = f32[8]{0:T(128)S(1)} all-reduce(f32[8]{0:T(128)S(1)} %reduce_sum.73), channel_id=1, replica_groups=mesh['patch'=128,'chan'=4] {'patch'}, use_global_device_ids=true, to_apply=%region_5.6 | all-reduce | flops 8 | bytes 64 | tf_op jit(solution)/shard_map/psum | solution.py:46
  640.5 1.2 convolution_reduce_fusion
  641.7 0.8 fusion.14
  642.6 116.3 %all-gather = bf16[4,320,64]{1,2,0:T(8,128)(2,1)S(1)} all-gather(bf16[1,320,64]{1,2,0:T(8,128)(2,1)S(1)} %fusion.14), channel_id=1, replica_groups=mesh['patch'=128,'chan'=4] {'chan'}, dimensions={0}, use_global_device_ids=true | all-gather | bytes 204800 | tf_op jit(solution)/shard_map/all_gather | solution.py:53
  759.2 1.3 convolution_convert_fusion.2
  760.6 1.3 convolution_convert_fusion.1
  762.1 1.3 convolution_convert_fusion
  764.0 12.9 reshape.91
  776.9 528.4 %all-gather.6.cloned.1.call-done = bf16[8192,256]{1,0:T(8,128)(2,1)} async-done(((bf16[64,256]{1,0:T(8,128)(2,1)}), bf16[8192,256]{1,0:T(8,128)(2,1)}) %all-gather.6.cloned.1.call-update) | async-done | bytes 4194320 | tf_op jit(solution)/shard_map/all_gather | solution.py:93
  1305.2 12.9 reshape.92
  1318.1 68.4 %while.14 = (s32[]{:T(128)}, f32[4,64]{1,0:T(4,128)S(1)}, f32[4,64,64]{1,2,0:T(8,128)S(1)}, f32[4,64]{1,0:T(4,128)S(1)}, s32[16]{0:T(128)S(1)}, /*index=5*/s32[]...) while((s32[]{:T(128)}, f32[4,64]{1,0:T(4,128)S(1)}, ...), condition=%wide.region_14.15_spmd, body=%wide.region_8.14_spmd.sunk | while | flops 34890256 | bytes 4054185 | solution.py:110
  1318.2 1.6 constant_dynamic-slice_fusion.3
  1320.1 0.6 dynamic_slice.16
  1321.6 0.4 copy.86
  1322.4 1.6 constant_dynamic-slice_fusion.3
  1324.3 0.6 dynamic_slice.16
  1325.9 0.4 copy.86
  1326.7 1.6 constant_dynamic-slice_fusion.3
  1328.6 0.6 dynamic_slice.16
  1330.2 0.4 copy.86
  1331.0 1.6 constant_dynamic-slice_fusion.3
  1332.9 0.6 dynamic_slice.16
  1334.5 0.4 copy.86
  1335.3 1.6 constant_dynamic-slice_fusion.3
  1337.2 0.6 dynamic_slice.16
  1339.5 1.6 constant_dynamic-slice_fusion.3
  1341.4 0.6 dynamic_slice.16
  1343.0 0.4 copy.86
  1343.8 1.6 constant_dynamic-slice_fusion.3
  1345.7 0.6 dynamic_slice.16
  1347.3 0.4 copy.86
  1348.1 1.6 constant_dynamic-slice_fusion.3
  1350.0 0.6 dynamic_slice.16
  1351.6 0.4 copy.86
  1352.4 1.6 constant_dynamic-slice_fusion.3
  1354.3 0.6 dynamic_slice.16
  1356.6 1.6 constant_dynamic-slice_fusion.3
  1358.5 0.6 dynamic_slice.16
  1360.1 0.4 copy.86
  1360.9 1.6 constant_dynamic-slice_fusion.3
  1362.8 0.6 dynamic_slice.16
  1364.4 0.4 copy.86
  1365.2 1.6 constant_dynamic-slice_fusion.3
  1367.1 0.6 dynamic_slice.16
  1369.5 1.6 constant_dynamic-slice_fusion.3
  1371.4 0.6 dynamic_slice.16
  1373.0 0.4 copy.86
  1373.8 1.6 constant_dynamic-slice_fusion.3
  1375.7 0.6 dynamic_slice.16
  1377.2 0.4 copy.86
  1378.0 1.6 constant_dynamic-slice_fusion.3
  1379.9 0.6 dynamic_slice.16
  1381.5 0.4 copy.86
  1382.3 1.6 constant_dynamic-slice_fusion.3
  1384.2 0.6 dynamic_slice.16
  1386.9 1.1 copy.67
  1388.0 135.4 %reduce-scatter.4.cloned.1.call-done = f32[320,64]{1,0:T(8,128)} async-done(((f32[1280,64]{1,0:T(8,128)}), f32[320,64]{1,0:T(8,128)}) %reduce-scatter.4.cloned.1.call-update) | async-done | bytes 81936
  1523.4 1.0 copy.68
  1524.4 0.6 fusion.12
  (202 shorter events, 21.1 us)
Async XLA Ops:
  7.2 1379.4 %copy-start = (bf16[256,1280]{1,0:T(8,128)(2,1)S(1)}, bf16[256,1280]{1,0:T(8,128)(2,1)}, u32[]{:S(2)}) copy-start(bf16[256,1280]{1,0:T(8,128)(2,1)} %param.21) | copy-start | bytes 1966084
  7.2 756.8 %all-gather.4.cloned.1.call-start = ((), (), s32[]{:S(2)}) async-start(), calls=%async_computation.1 | async-start | bytes 4227072 | tf_op jit(solution)/shard_map/all_gather | solution.py:92
  7.9 1297.3 %all-gather.6.cloned.1.call-start = ((), (), s32[]{:S(2)}) async-start(), calls=%async_computation.2 | async-start | bytes 4227072 | tf_op jit(solution)/shard_map/all_gather | solution.py:93
  8.7 1514.7 %reduce-scatter.4.cloned.1.call-start = ((), (), s32[]{:S(2)}) async-start(), calls=%async_computation.3 | async-start | bytes 819200
  762.0 556.2 %copy-start.2 = (bf16[64,256]{1,0:T(8,128)(2,1)}, bf16[64,256]{1,0:T(8,128)(2,1)S(1)}, u32[]{:S(2)}) copy-start(bf16[64,256]{1,0:T(8,128)(2,1)S(1)} %convolution_convert_fusion.1) | copy-start | bytes 98308
  763.4 554.7 %copy-start.3 = (bf16[64,256]{1,0:T(8,128)(2,1)}, bf16[64,256]{1,0:T(8,128)(2,1)S(1)}, u32[]{:S(2)}) copy-start(bf16[64,256]{1,0:T(8,128)(2,1)S(1)} %convolution_convert_fusion) | copy-start | bytes 98308
  1318.1 206.3 %copy-start.1 = (bf16[64,320]{1,0:T(8,128)(2,1)S(1)}, bf16[64,320]{1,0:T(8,128)(2,1)}, u32[]{:S(2)}) copy-start(bf16[64,320]{1,0:T(8,128)(2,1)} %param.13) | copy-start | bytes 122884
Sparse Core Ops, SparseCore 0:
  10.1 606.6 all-gather.3
  618.9 686.3 all-gather.5
  1388.1 135.2 reduce-scatter.3
where the time goes:
time: 1530 us
  blocking collectives  745 us (49%)
  waiting for transfers between devices  665 us (43%)
  local copies, waits for them, and re-layouts  69.9 us (5%)
  matrix products  15.5 us (1%)
    all_gather x1, waiting for transfers between devices, local(): value_piece = lax.all_gather(stale_values, 'patch', axis=0, tiled=True)  528 us
    psum x1, blocking collectives, local(): group_total = lax.psum(jnp.sum(values, axis=(0, 2)), 'patch')  319 us
    psum x1, blocking collectives, local(): spread = lax.psum(jnp.sum(centered * centered, axis=(0, 2)), 'patch')  309 us
    unnamed x4, waiting for transfers between devices  137 us
    all_gather x1, blocking collectives, local(): shard_piece = lax.all_gather(normed, 'chan', axis=1, tiled=True)  116 us
    dynamic_slice x48, local copies, waits for them, and re-layouts, local(): lax.scan(advance, start_state, (key_steps, value_steps, step_ids))  40.8 us
  transfers between devices with their start and end apart: 3, of which 2 were waited for; matrix products, arithmetic and copies ran while one was open for 1% of the time, Pallas kernels for 0%

commit v1 on v0

--- a/solution.py
+++ b/solution.py
@@ -7,6 +7,16 @@
 D = 1280
 HEAD_DIM = 64
 GROUPS = 32
+
+
+def begin_the_loads(block_in, d0):
+    state_now = jax.lax.all_to_all(
+        jnp.stack([block_in for _ in range(jax.lax.axis_size("patch"))], 0),
+        axis_name="patch",
+        split_axis=0,
+        concat_axis=0,
+    )
+    return jnp.concatenate(state_now, d0)
 
 
 def timestep_shift(timestep, w_time):
@@ -90,7 +100,7 @@
     )
     start_state = (home_max[..., 0], home_num[:, :, 0], home_den[..., 0])
     key_piece = lax.all_gather(stale_keys, "patch", axis=0, tiled=True)
-    value_piece = lax.all_gather(stale_values, "patch", axis=0, tiled=True)
+    value_piece = begin_the_loads(stale_values, 0)
     slab_count = key_piece.shape[0] // rows_here
     per_step = math.gcd(slab_count, 8)
     key_steps = key_piece.reshape(slab_count // per_step, per_step, rows_here, heads_here, HEAD_DIM)

time: 1530 us -> 1010 us (0.66)
  waiting for transfers between devices: 665 us -> 44.1 us
  blocking collectives: 745 us -> 824 us
  starting transfers between devices: 0.11 us -> 18.4 us
    all_gather x1 -> x0, waiting for transfers between devices: 528 us -> none  [local(): value_piece = lax.all_gather(stale_values, 'patch', axis=0, tiled=True)]
    unnamed x4 -> x3, waiting for transfers between devices: 137 us -> 44.1 us
    psum x1, blocking collectives: 319 us -> 399 us  [local(): group_total = lax.psum(jnp.sum(values, axis=(0, 2)), 'patch')]
    all_to_all x0 -> x1, starting transfers between devices: none -> 18.3 us  [begin_the_loads(): jax.lax.all_to_all(jnp.stack([block_in for _ in range(jax.lax.axis_size('...]
    another operation x2 -> x4, local copies, waits for them, and re-layouts: 0.21 us -> 16.5 us  [the longest x1 12.9 us: local(): value_piece.reshape(slab_count // per_step, per_step, rows_here, heads_he...]
  transfers between devices with their start and end apart: 3 -> 3, of which waited for: 2 -> 1; matrix products, arithmetic and copies ran while one was open for 1% -> 2% of each run, Pallas kernels for 0% -> 0%
where the time goes in v1:
time: 1010 us
  blocking collectives  824 us (82%)
  local copies, waits for them, and re-layouts  73.3 us (7%)
  waiting for transfers between devices  44.1 us (4%)
  starting transfers between devices  18.4 us (2%)
  between operations  15 us (1%)
  matrix products  11.2 us (1%)
  loops' own time  10.3 us (1%)
    psum x1, blocking collectives, local(): group_total = lax.psum(jnp.sum(values, axis=(0, 2)), 'patch')  399 us
    psum x1, blocking collectives, local(): spread = lax.psum(jnp.sum(centered * centered, axis=(0, 2)), 'patch')  314 us
    all_gather x1, blocking collectives, local(): shard_piece = lax.all_gather(normed, 'chan', axis=1, tiled=True)  112 us
    unnamed x3, waiting for transfers between devices  44.1 us
    dynamic_slice x48, local copies, waits for them, and re-layouts, local(): lax.scan(advance, start_state, (key_steps, value_steps, step_ids))  40.8 us
  transfers between devices with their start and end apart: 3, of which 1 were waited for; matrix products, arithmetic and copies ran while one was open for 2% of the time, Pallas kernels for 0%

profile of v1, /device:TPU:1, one launch (start us, length us, event | category | flops | bytes accessed | tf_op | source)
XLA Modules:
  0.0 1005.3 jit_solution(5733420351303370536)
XLA Ops:
  7.3 3.4 stack.2
  10.6 18.3 %all-to-all-start = ((bf16[128,64,256]{2,1,0:T(8,128)(2,1)}), bf16[128,64,256]{2,1,0:T(8,128)(2,1)}, u32[]{:S(2)}, u32[]{:S(2)}) async-start(bf16[128,64,256]{2,1,0:T(8,128)(2,1)} %stack.2), calls=%async_computation | async-start | bytes 8388608 | tf_op jit(solution)/shard_map/all_to_all | solution.py:13
  29.0 0.7 all-gather.3.cloned.1.call-update
  30.0 399.0 %psum.14 = f32[8]{0:T(128)S(1)} all-reduce(f32[8]{0:T(128)S(1)} %reduce_sum.70), channel_id=1, replica_groups=mesh['patch'=128,'chan'=4] {'patch'}, use_global_device_ids=true, to_apply=%region_2.0 | all-reduce | flops 8 | bytes 64 | tf_op jit(solution)/shard_map/psum | solution.py:53
  429.4 313.6 %psum.15 = f32[8]{0:T(128)S(1)} all-reduce(f32[8]{0:T(128)S(1)} %reduce_sum.73), channel_id=1, replica_groups=mesh['patch'=128,'chan'=4] {'patch'}, use_global_device_ids=true, to_apply=%region_5.6 | all-reduce | flops 8 | bytes 64 | tf_op jit(solution)/shard_map/psum | solution.py:56
  744.3 111.6 %all-gather = bf16[4,320,64]{1,2,0:T(8,128)(2,1)S(1)} all-gather(bf16[1,320,64]{1,2,0:T(8,128)(2,1)S(1)} %fusion.14), channel_id=1, replica_groups=mesh['patch'=128,'chan'=4] {'chan'}, dimensions={0}, use_global_device_ids=true | all-gather | bytes 204800 | tf_op jit(solution)/shard_map/all_gather | solution.py:63
  857.7 12.9 %reshape_reshape.3 = bf16[16,8,64,4,64]{4,3,2,1,0:T(4,128)(2,1)} reshape(bf16[128,64,256]{2,1,0:T(8,128)(2,1)} %all-to-all-done) | data formatting | bytes 8388608 | tf_op jit(solution)/shard_map/reshape;reshape | solution.py:107
  870.6 12.9 %reshape.89 = bf16[16,8,64,4,64]{4,3,2,1,0:T(4,128)(2,1)} reshape(bf16[8192,256]{1,0:T(8,128)(2,1)} %all-gather.3.cloned.1.call-done) | data formatting | bytes 8388608 | tf_op jit(solution)/shard_map/reshape | solution.py:106
  883.5 68.4 %while.14 = (s32[]{:T(128)}, f32[4,64]{1,0:T(4,128)S(1)}, f32[4,64,64]{1,2,0:T(8,128)S(1)}, f32[4,64]{1,0:T(4,128)S(1)}, s32[16]{0:T(128)S(1)}, /*index=5*/s32[]...) while((s32[]{:T(128)}, f32[4,64]{1,0:T(4,128)S(1)}, ...), condition=%wide.region_14.15_spmd, body=%wide.region_8.14_spmd.sunk | while | flops 34890256 | bytes 4054185 | solution.py:120
  883.5 1.6 constant_dynamic-slice_fusion.3
  885.1 0.3 fusion.35
  885.4 0.6 dynamic_slice.16
  887.0 0.4 copy.81
  887.8 1.6 constant_dynamic-slice_fusion.3
  889.4 0.3 fusion.35
  889.7 0.6 dynamic_slice.16
  891.3 0.4 copy.81
  892.1 1.6 constant_dynamic-slice_fusion.3
  894.0 0.6 dynamic_slice.16
  895.6 0.4 copy.81
  896.3 1.6 constant_dynamic-slice_fusion.3
  898.2 0.6 dynamic_slice.16
  899.8 0.4 copy.81
  900.6 1.6 constant_dynamic-slice_fusion.3
  902.2 0.3 fusion.35
  902.5 0.6 dynamic_slice.16
  904.1 0.4 copy.81
  904.9 1.6 constant_dynamic-slice_fusion.3
  906.8 0.6 dynamic_slice.16
  908.4 0.4 copy.81
  909.2 1.6 constant_dynamic-slice_fusion.3
  911.1 0.6 dynamic_slice.16
  912.7 0.4 copy.81
  913.5 1.6 constant_dynamic-slice_fusion.3
  915.4 0.6 dynamic_slice.16
  916.9 0.4 copy.81
  917.7 1.6 constant_dynamic-slice_fusion.3
  919.6 0.6 dynamic_slice.16
  921.2 0.4 copy.81
  922.0 1.6 constant_dynamic-slice_fusion.3
  923.9 0.6 dynamic_slice.16
  925.5 0.4 copy.81
  926.3 1.6 constant_dynamic-slice_fusion.3
  928.2 0.6 dynamic_slice.16
  929.8 0.4 copy.81
  930.6 1.6 constant_dynamic-slice_fusion.3
  932.5 0.6 dynamic_slice.16
  934.1 0.4 copy.81
  934.8 1.6 constant_dynamic-slice_fusion.3
  936.8 0.6 dynamic_slice.16
  938.3 0.4 copy.81
  939.1 1.6 constant_dynamic-slice_fusion.3
  941.0 0.6 dynamic_slice.16
  942.6 0.4 copy.81
  943.4 1.6 constant_dynamic-slice_fusion.3
  945.3 0.6 dynamic_slice.16
  946.9 0.4 copy.81
  947.7 1.6 constant_dynamic-slice_fusion.3
  949.6 0.6 dynamic_slice.16
  951.2 0.4 copy.81
  952.2 1.1 copy.62
  953.3 43.4 %reduce-scatter.4.cloned.1.call-done = f32[320,64]{1,0:T(8,128)} async-done(((f32[1280,64]{1,0:T(8,128)}), f32[320,64]{1,0:T(8,128)}) %reduce-scatter.4.cloned.1.call-update) | async-done | bytes 81936
  996.8 1.0 copy.63
  997.8 0.6 fusion.12
  (214 shorter events, 19.8 us)
Async XLA Ops:
  7.2 944.8 %copy-start = (bf16[256,1280]{1,0:T(8,128)(2,1)S(1)}, bf16[256,1280]{1,0:T(8,128)(2,1)}, u32[]{:S(2)}) copy-start(bf16[256,1280]{1,0:T(8,128)(2,1)} %param.21) | copy-start | bytes 1966084
  7.2 22.5 %copy-start.1 = (bf16[64,320]{1,0:T(8,128)(2,1)S(1)}, bf16[64,320]{1,0:T(8,128)(2,1)}, u32[]{:S(2)}) copy-start(bf16[64,320]{1,0:T(8,128)(2,1)} %param.13) | copy-start | bytes 122884
  7.2 736.8 %copy-start.5 = (bf16[320,320]{1,0:T(8,128)(2,1)S(1)}, bf16[320,320]{1,0:T(8,128)(2,1)}, u32[]{:S(2)}) copy-start(bf16[320,320]{1,0:T(8,128)(2,1)} %param.17) | copy-start | bytes 614404
  7.2 737.0 %copy-start.9 = (f32[320]{0:T(512)S(1)}, f32[320]{0:T(512)}, u32[]{:S(2)}) copy-start(f32[320]{0:T(512)} %param.15) | copy-start | bytes 3844
  7.2 737.0 %copy-start.8 = (f32[320]{0:T(512)S(1)}, f32[320]{0:T(512)}, u32[]{:S(2)}) copy-start(f32[320]{0:T(512)} %param.16) | copy-start | bytes 3844
  7.2 849.0 %copy-start.2 = (bf16[1280,256]{1,0:T(8,128)(2,1)S(1)}, bf16[1280,256]{1,0:T(8,128)(2,1)}, u32[]{:S(2)}) copy-start(bf16[1280,256]{1,0:T(8,128)(2,1)} %param.18) | copy-start | bytes 1966084
  7.2 849.3 %copy-start.3 = (bf16[1280,256]{1,0:T(8,128)(2,1)S(1)}, bf16[1280,256]{1,0:T(8,128)(2,1)}, u32[]{:S(2)}) copy-start(bf16[1280,256]{1,0:T(8,128)(2,1)} %param.19) | copy-start | bytes 1966084
  7.2 849.7 %copy-start.4 = (bf16[1280,256]{1,0:T(8,128)(2,1)S(1)}, bf16[1280,256]{1,0:T(8,128)(2,1)}, u32[]{:S(2)}) copy-start(bf16[1280,256]{1,0:T(8,128)(2,1)} %param.20) | copy-start | bytes 1966084
  10.6 847.1 %all-to-all-start = ((bf16[128,64,256]{2,1,0:T(8,128)(2,1)}), bf16[128,64,256]{2,1,0:T(8,128)(2,1)}, u32[]{:S(2)}, u32[]{:S(2)}) async-start(bf16[128,64,256]{2,1,0:T(8,128)(2,1)} %stack.2), calls=%async_computation | async-start | bytes 8388608 | tf_op jit(solution)/shard_map/all_to_all | solution.py:13
  28.9 841.7 %all-gather.3.cloned.1.call-start = ((), (), s32[]{:S(2)}) async-start(), calls=%async_computation.2 | async-start | bytes 4227072 | tf_op jit(solution)/shard_map/all_gather | solution.py:102
  29.7 967.1 %reduce-scatter.4.cloned.1.call-start = ((), (), s32[]{:S(2)}) async-start(), calls=%async_computation.3 | async-start | bytes 819200
  856.8 26.7 %copy-start.6 = (bf16[64,256]{1,0:T(8,128)(2,1)}, bf16[64,256]{1,0:T(8,128)(2,1)S(1)}, u32[]{:S(2)}) copy-start(bf16[64,256]{1,0:T(8,128)(2,1)S(1)} %convolution_convert_fusion.1) | copy-start | bytes 98308
  857.2 26.3 %copy-start.7 = (bf16[64,256]{1,0:T(8,128)(2,1)}, bf16[64,256]{1,0:T(8,128)(2,1)S(1)}, u32[]{:S(2)}) copy-start(bf16[64,256]{1,0:T(8,128)(2,1)S(1)} %convolution_convert_fusion) | copy-start | bytes 98308
Sparse Core Ops, SparseCore 0:
  31.8 633.7 all-gather.2
  953.5 43.2 reduce-scatter.3
